TPU v7x, 32 devices: a whole 2x2x4 slice. The times are simulated.
32 devices in a mesh: seq: 4 (over y, core), batch: 8 (over z, x).
Axes of the slice: x: 2, y: 2, z: 4, core: 2. Of those that a mesh axis runs over, the one named last changes fastest.
Arguments:
- inputs: bfloat16 [8, 512, 768], P('batch', 'seq'), may hold values from -6 to 6
- cotangent: bfloat16 [8, 512, 768], P('batch', 'seq'), may hold values from -6 to 6
- weight: bfloat16 [768, 2304], replicated, may hold values from -0.125 to 0.125
Outputs:
- grad_input: bfloat16 [8, 512, 768], P('batch', 'seq')
- grad_weight: float32 [768, 2304], P('seq', 'batch')
All inputs are finite; a program needn't handle non-finite values.
Results may differ from a plain program's by a relative error of at most 0.0026.
Values may be sent and summed in bfloat16 or wider, within the bound.
No kernel may reach another device: no remote copies, remote signals or barrier semaphores. Data moves between devices by JAX's collectives and lax.ppermute only.
A program may use at most 64 MiB of HBM per device.

v0:
```python
import math
import jax
import jax.numpy as jnp
from jax import lax
from jax.experimental.layout import Layout, with_layout_constraint
from jax.sharding import PartitionSpec as P

KW = 3
TAP_SPACING = 64
HEADROOM = 12.0
TAG = 16


def extended_2(x, sides, width):
    for axis, dim in sides:
        peers, length = (lax.axis_size(axis), x.shape[dim])
        up = [(i, (i + 1) % peers) for i in range(peers - 1)]
        down = [(j, i) for i, j in up]
        last = lax.slice_in_dim(x, length - width, length, axis=dim)
        first = lax.slice_in_dim(x, 0, width, axis=dim)
        before = lax.ppermute(last, axis, up)
        after = lax.ppermute(first, axis, down)
        x = jnp.concatenate([before, x, after], axis=dim)
    return x


def gelu_factors(values):
    normal_cdf = 0.5 * (1.0 + jax.scipy.special.erf(values / math.sqrt(2.0)))
    density = jnp.exp(-0.5 * values * values) / math.sqrt(2.0 * math.pi)
    return (values * normal_cdf, normal_cdf + values * density)


def exponent_of(values):
    flat = values.reshape(-1, values.shape[-1])
    biggest = jnp.max(jnp.abs(flat), axis=0, keepdims=True)
    return jnp.floor(jnp.log2(jnp.maximum(biggest, 1e-30)))


def encode(values, exponent):
    flat = values.reshape(-1, values.shape[-1])
    scaled = (flat * jnp.exp2(HEADROOM - exponent)).astype(jnp.float16)
    tag = jnp.broadcast_to(exponent.astype(jnp.float16), (TAG, flat.shape[-1]))
    return with_layout_constraint(jnp.concatenate([scaled, tag], axis=0), Layout((0, 1)))


def decode(packed, shape):
    exponent = packed[-TAG : 1 - TAG].astype(jnp.float32)
    values = packed[:-TAG].astype(jnp.float32) * jnp.exp2(exponent - HEADROOM)
    return values.reshape(shape)


def send(values, perm, exponent):
    arrived = lax.ppermute(encode(values, exponent), "batch", perm)
    return decode(with_layout_constraint(arrived, Layout((0, 1))), values.shape)


def reduce_over_batch(columns):
    count = lax.axis_size("batch")
    outer = count // 2
    me = lax.axis_index("batch")
    x = me % 2
    z = me // 2
    pairs = [(i, i ^ 1) for i in range(count)]
    blocks = columns.reshape(outer, 2, -1, columns.shape[1])
    mine = lax.dynamic_index_in_dim(blocks, x, axis=1, keepdims=False)
    theirs = lax.dynamic_index_in_dim(blocks, 1 - x, axis=1, keepdims=False)
    half = outer // 2
    received = jnp.concatenate(
        [
            send(theirs[:half], pairs, exponent_of(theirs[:half])),
            send(theirs[half:], pairs, exponent_of(theirs[half:])),
        ],
        axis=0,
    )
    summed = with_layout_constraint(mine + received, Layout((0, 1, 2)))
    spread = exponent_of(summed)
    total = lax.dynamic_index_in_dim(summed, z, axis=0, keepdims=False)
    for shift in sorted(range(1, outer), key=lambda d: (min(d, outer - d), -d)):
        target = lax.dynamic_index_in_dim(summed, (z + shift) % outer, axis=0, keepdims=False)
        perm = [(2 * q + p, 2 * ((q + shift) % outer) + p) for q in range(outer) for p in range(2)]
        total = total + send(target, perm, spread)
    return with_layout_constraint(total, Layout((0, 1))).T


def gather_over_seq(block, cot, width):
    count = lax.axis_size("seq")
    me = lax.axis_index("seq")
    bits = count.bit_length() - 1
    rows = cot.shape[0]
    last = cot[rows - width :]
    first = cot[:width]
    odd = me % 2 == 1
    stack = block[None]
    for bit in reversed(range(1, bits)):
        pairs = [(i, i ^ 1 << bit) for i in range(count)]
        stack = jnp.concatenate([stack, lax.ppermute(stack, "seq", pairs)], axis=0)
    piece = jnp.where(odd, first, last)
    outgoing = jnp.concatenate([stack.reshape(-1, block.shape[-1]), piece], axis=0)
    incoming = lax.ppermute(outgoing, "seq", [(i, i ^ 1) for i in range(count)])
    near = incoming[-width:]
    stack = jnp.concatenate([stack, incoming[:-width].reshape(stack.shape)], axis=0)
    across = [(i, i + 1) for i in range(1, count - 1, 2)] + [(i, i - 1) for i in range(2, count, 2)]
    far = lax.ppermute(jnp.where(odd, last, first), "seq", across)
    before = jnp.where(odd, near, far)
    after = jnp.where(odd, far, near)
    extended = jnp.concatenate([before, cot, after], axis=0)
    reverse = jnp.array([int(format(v, "0%db" % bits)[::-1], 2) for v in range(count)], jnp.int32)
    order = reverse[jnp.bitwise_xor(me, jnp.arange(count, dtype=jnp.int32))]
    return (jnp.take(stack, order, axis=0).reshape(-1, block.shape[-1]), extended)


def body(inputs, cotangent, weight):
    middle_offset = KW // 2
    reach = middle_offset * TAP_SPACING
    length = inputs.shape[1]
    in_width = inputs.shape[2]
    values = inputs[0].astype(jnp.float32)
    activation, deriv = gelu_factors(values)
    act = activation.astype(jnp.bfloat16)
    seq_count = lax.axis_size("seq")
    batch_count = lax.axis_size("batch")
    counted = batch_count * inputs.shape[0] * length * seq_count
    factor = 1.0 / math.sqrt(float(counted))
    channels = cotangent[0].T.reshape(seq_count, -1, length)
    arrived = lax.all_to_all(channels, "seq", 0, 0, tiled=True)
    own_rows = arrived.shape[1]
    owned = jnp.transpose(arrived, (1, 0, 2)).reshape(own_rows, -1)
    if seq_count >= 2 and seq_count & seq_count - 1 == 0:
        whole_act, extended = gather_over_seq(act, cotangent[0], reach)
    else:
        whole_act = lax.all_gather(act[None], "seq", axis=1, tiled=True)[0]
        extended = extended_2(cotangent, (("seq", 1),), reach)[0]
    count = whole_act.shape[0]
    act_padded = jnp.pad(whole_act, ((reach, reach), (0, 0)))
    updated = []
    for tap_index in range(KW):
        window = lax.slice_in_dim(
            act_padded, tap_index * TAP_SPACING, tap_index * TAP_SPACING + count, axis=0
        )
        updated.append(
            lax.dot_general(
                window, owned, (((0,), (1,)), ((), ())), preferred_element_type=jnp.float32
            )
        )
    local_columns = jnp.concatenate(updated, axis=0) * factor
    local_columns = with_layout_constraint(local_columns, Layout((0, 1)))
    local_columns, extended, deriv = lax.optimization_barrier((local_columns, extended, deriv))
    grad_act = jnp.zeros((length, in_width), jnp.float32)
    for tap_index in range(KW):
        window_start = (2 * middle_offset - tap_index) * TAP_SPACING
        window = lax.slice_in_dim(extended, window_start, window_start + length, axis=0)
        grad_act = grad_act + jnp.dot(
            window,
            weight[:, tap_index * in_width : (tap_index + 1) * in_width],
            preferred_element_type=jnp.float32,
        )
    grad_input = (grad_act * deriv).astype(jnp.bfloat16)[None]
    if batch_count == 8:
        grad_weight = reduce_over_batch(local_columns)
    else:
        pieces = local_columns.reshape(batch_count, -1, own_rows)
        swapped = lax.all_to_all(pieces, "batch", split_axis=0, concat_axis=0, tiled=True)
        grad_weight = jnp.sum(swapped, axis=0).T
    return (grad_input, grad_weight)


def solution(mesh):
    placed = (P("batch", "seq", None), P("batch", "seq", None), P())
    return jax.shard_map(
        body,
        mesh=mesh,
        in_specs=placed,
        out_specs=(P("batch", "seq", None), P("seq", "batch")),
        check_vma=False,
    )
```

profile of v0, /device:TPU:0, one launch (start us, length us, event | category | flops | bytes accessed | tf_op | source)
XLA Modules:
  0.0 54.8 jit_solution(10538124624055871205)
XLA Ops:
  0.6 1.1 %fusion.28 = bf16[1,128,768]{2,1,0:T(8,128)(2,1)S(1)} fusion(bf16[1,128,768]{2,1,0:T(8,128)(2,1)} %param.4), kind=kLoop, calls=%fused_computation.47 | loop fusion | flops 589824 | bytes 393216 | tf_op jit(solution)/shard_map/convert_element_type | solution.py:119
  1.7 3.0 %collective-permute-start = (bf16[1,128,768]{2,1,0:T(8,128)(2,1)S(1)}, bf16[1,128,768]{2,1,0:T(8,128)(2,1)S(1)}, u32[]{:S(2)}, u32[]{:S(2)}) collective-permute-start(bf16[1,128,768]{2,1,0:T(8,128)(2,1)S(1)} %fusion.28), channel_id=1, source_target_pairs={{0,16},{8,24},{16,0},{24,8},{1,17},{9,25},{17,1},{25,9},{2,18},{10... | collective-permute-start | bytes 589832 | tf_op jit(solution)/shard_map/ppermute | solution.py:96
  4.8 1.7 %copy.13 = bf16[768,128]{1,0:T(8,128)(2,1)} copy(bf16[768,128]{0,1:T(8,128)(2,1)} %bitcast.121) | data formatting | bytes 393216 | tf_op jit(solution)/shard_map/transpose | solution.py:124
  6.5 3.4 %all-to-all-start = ((bf16[4,192,128]{2,1,0:T(8,128)(2,1)}), bf16[4,192,128]{2,1,0:T(8,128)(2,1)S(1)}, u32[]{:S(2)}, u32[]{:S(2)}) async-start(bf16[4,192,128]{2,1,0:T(8,128)(2,1)} %bitcast.10), calls=%async_computation | async-start | bytes 393216 | tf_op jit(solution)/shard_map/all_to_all | solution.py:125
  9.9 1.0 %select_bitcast_fusion = (bf16[64,768]{1,0:T(8,128)(2,1)S(1)}, bf16[64,768]{1,0:T(8,128)(2,1)S(1)}) fusion(pred[]{:T(512)S(6)} %eq.9, bf16[1,128,768]{2,1,0:T(8,128)(2,1)} %param.5), kind=kLoop, calls=%fused_computation.76 | loop fusion | flops 98304 | bytes 393217 | tf_op jit(solution)/shard_map/jit(_where)/select_n | solution.py:103
  10.8 0.7 %collective-permute-start.2 = (bf16[64,768]{1,0:T(8,128)(2,1)S(1)}, bf16[64,768]{1,0:T(8,128)(2,1)S(1)}, u32[]{:S(2)}, u32[]{:S(2)}) collective-permute-start(bf16[64,768]{1,0:T(8,128)(2,1)S(1)} %get-tuple-element.25), channel_id=1, source_target_pairs={{8,16},{16,8},{9,17},{17,9},{10,18},{18,10},{11,19},{19,11},{12,20... | collective-permute-start | bytes 294920 | tf_op jit(solution)/shard_map/ppermute | solution.py:103
  11.5 1.3 %gather_fusion = s32[4]{0:T(128)S(1)} fusion(s32[4]{0:T(128)} %constant.123.clone, s32[1024]{0:T(1024)S(1)} %pad_clamp_fusion.1), kind=kCustom, calls=%fused_computation | custom fusion | bytes 48 | tf_op jit(solution)/shard_map/gather | solution.py:108
  13.0 3.4 %collective-permute-start.1 = (bf16[320,768]{1,0:T(8,128)(2,1)S(1)}, bf16[320,768]{1,0:T(8,128)(2,1)S(1)}, u32[]{:S(2)}, u32[]{:S(2)}) collective-permute-start(bf16[320,768]{1,0:T(8,128)(2,1)S(1)} %pad_maximum_fusion.1), channel_id=1, source_target_pairs={{0,8},{8,0},{16,24},{24,16},{1,9},{9,1},{17,25},{25,17},{2,10},{10... | collective-permute-start | bytes 1474568 | tf_op jit(solution)/shard_map/ppermute | solution.py:99
  16.6 1.2 %collective-permute-done.1 = bf16[320,768]{1,0:T(8,128)(2,1)S(1)} collective-permute-done((bf16[320,768]{1,0:T(8,128)(2,1)S(1)}, bf16[320,768]{1,0:T(8,128)(2,1)S(1)}, u32[]{:S(2)}, u32[]{:S(2)}) %collective-permute-start.1) | collective-permute-done | bytes 491552 | tf_op jit(solution)/shard_map/ppermute | solution.py:99
  18.0 0.6 %gather_fusion.1 = bf16[4,128,768]{2,1,0:T(8,128)(2,1)S(1)} fusion(bf16[4,128,768]{2,1,0:T(8,128)(2,1)S(1)} %pad_maximum_fusion, s32[1024]{0:T(1024)S(1)} %pad_clamp_fusion), kind=kCustom, calls=%fused_computation.1 | custom fusion | bytes 1572880 | tf_op jit(solution)/shard_map/jit(_take)/gather | solution.py:109
  18.7 0.5 convolution_bitcast_fusion
  19.7 0.4 fusion.11
  20.3 0.7 %copy-done = bf16[1,128,768]{2,1,0:T(8,128)(2,1)S(1)} copy-done((bf16[1,128,768]{2,1,0:T(8,128)(2,1)S(1)}, bf16[1,128,768]{2,1,0:T(8,128)(2,1)}, u32[]{:S(2)}) %copy-start) | copy-done | bytes 196632
  21.4 1.6 %collective-permute-start.4 = (f16[592,192]{1,0:T(8,128)(2,1)S(1)}, f16[592,192]{1,0:T(8,128)(2,1)S(1)}, u32[]{:S(2)}, u32[]{:S(2)}) collective-permute-start(f16[592,192]{1,0:T(8,128)(2,1)S(1)} %pad_maximum_fusion.5), channel_id=1, source_target_pairs={{0,1},{1,0},{2,3},{3,2},{4,5},{5,4},{6,7},{7,6},{8,9},{9,8},{10,11... | collective-permute-start | bytes 681992 | tf_op jit(solution)/shard_map/ppermute | solution.py:53
  23.2 0.6 %collective-permute-start.3 = (f16[592,192]{1,0:T(8,128)(2,1)S(1)}, f16[592,192]{1,0:T(8,128)(2,1)S(1)}, u32[]{:S(2)}, u32[]{:S(2)}) collective-permute-start(f16[592,192]{1,0:T(8,128)(2,1)S(1)} %pad_maximum_fusion.4), channel_id=1, source_target_pairs={{0,1},{1,0},{2,3},{3,2},{4,5},{5,4},{6,7},{7,6},{8,9},{9,8},{10,11... | collective-permute-start | bytes 681992 | tf_op jit(solution)/shard_map/ppermute | solution.py:53
  24.4 7.1 %collective-permute-done.4 = f16[592,192]{1,0:T(8,128)(2,1)S(1)} collective-permute-done((f16[592,192]{1,0:T(8,128)(2,1)S(1)}, f16[592,192]{1,0:T(8,128)(2,1)S(1)}, u32[]{:S(2)}, u32[]{:S(2)}) %collective-permute-start.4) | collective-permute-done | bytes 227360 | tf_op jit(solution)/shard_map/ppermute | solution.py:53
  31.5 5.9 %collective-permute-done.3 = f16[592,192]{1,0:T(8,128)(2,1)S(1)} collective-permute-done((f16[592,192]{1,0:T(8,128)(2,1)S(1)}, f16[592,192]{1,0:T(8,128)(2,1)S(1)}, u32[]{:S(2)}, u32[]{:S(2)}) %collective-permute-start.3) | collective-permute-done | bytes 227360 | tf_op jit(solution)/shard_map/ppermute | solution.py:53
  38.0 2.7 %collective-permute-start.7 = (f16[304,192]{1,0:T(8,128)(2,1)S(1)}, f16[304,192]{1,0:T(8,128)(2,1)S(1)}, u32[]{:S(2)}, u32[]{:S(2)}) collective-permute-start(f16[304,192]{1,0:T(8,128)(2,1)S(1)} %get-tuple-element.29), channel_id=1, source_target_pairs={{0,4},{1,5},{2,6},{3,7},{4,0},{5,1},{6,2},{7,3},{8,12},{9,13},{10,... | collective-permute-start | bytes 350216 | tf_op jit(solution)/shard_map/ppermute | solution.py:53
  40.7 1.0 %fusion.8 = bf16[1,128,768]{2,1,0:T(8,128)(2,1)} fusion(f32[128,768]{1,0:T(8,128)S(1)} %fusion.24, f32[128,768]{1,0:T(8,128)S(1)} %convolution_add_fusion.1, bf16[768,2304]{1,0:T(8,128)(2,1)S(1)} %copy-done.1, bf16[256,768]{1,0:T(8,128)(2,1)S(1)} %pad_maximum_fusion.3), kind=kOutput, calls=%fused_computation.14 | convolution fusion | flops 151289856 | bytes 2359296 | tf_op jit(solution)/shard_map/dot_general | solution.py:152
  41.7 1.6 %collective-permute-start.6 = (f16[304,192]{1,0:T(8,128)(2,1)S(1)}, f16[304,192]{1,0:T(8,128)(2,1)S(1)}, u32[]{:S(2)}, u32[]{:S(2)}) collective-permute-start(f16[304,192]{1,0:T(8,128)(2,1)S(1)} %get-tuple-element.28), channel_id=1, source_target_pairs={{0,2},{1,3},{2,4},{3,5},{4,6},{5,7},{6,0},{7,1},{8,10},{9,11},{10,... | collective-permute-start | bytes 350216 | tf_op jit(solution)/shard_map/ppermute | solution.py:53
  43.3 2.3 %collective-permute-start.5 = (f16[304,192]{1,0:T(8,128)(2,1)S(1)}, f16[304,192]{1,0:T(8,128)(2,1)S(1)}, u32[]{:S(2)}, u32[]{:S(2)}) collective-permute-start(f16[304,192]{1,0:T(8,128)(2,1)S(1)} %get-tuple-element.27), channel_id=1, source_target_pairs={{0,6},{1,7},{2,0},{3,1},{4,2},{5,3},{6,4},{7,5},{8,14},{9,15},{10,... | collective-permute-start | bytes 350216 | tf_op jit(solution)/shard_map/ppermute | solution.py:53
  45.5 6.8 %collective-permute-done.7 = f16[304,192]{1,0:T(8,128)(2,1)S(1)} collective-permute-done((f16[304,192]{1,0:T(8,128)(2,1)S(1)}, f16[304,192]{1,0:T(8,128)(2,1)S(1)}, u32[]{:S(2)}, u32[]{:S(2)}) %collective-permute-start.7) | collective-permute-done | bytes 116768 | tf_op jit(solution)/shard_map/ppermute | solution.py:53
  52.4 1.4 %collective-permute-done.5 = f16[304,192]{1,0:T(8,128)(2,1)S(1)} collective-permute-done((f16[304,192]{1,0:T(8,128)(2,1)S(1)}, f16[304,192]{1,0:T(8,128)(2,1)S(1)}, u32[]{:S(2)}, u32[]{:S(2)}) %collective-permute-start.5) | collective-permute-done | bytes 116768 | tf_op jit(solution)/shard_map/ppermute | solution.py:53
  53.9 0.9 %copy.20 = f32[192,288]{1,0:T(8,128)} copy(f32[192,288]{0,1:T(8,128)S(1)} %fusion.37) | data formatting | bytes 442368
  (49 shorter events, 3.2 us)
Async XLA Ops:
  0.6 15.8 %copy-start.2 = (bf16[1,128,768]{2,1,0:T(8,128)(2,1)S(1)}, bf16[1,128,768]{2,1,0:T(8,128)(2,1)}, u32[]{:S(2)}) copy-start(bf16[1,128,768]{2,1,0:T(8,128)(2,1)} %param.4) | copy-start | bytes 589828
  1.7 11.1 %collective-permute-start = (bf16[1,128,768]{2,1,0:T(8,128)(2,1)S(1)}, bf16[1,128,768]{2,1,0:T(8,128)(2,1)S(1)}, u32[]{:S(2)}, u32[]{:S(2)}) collective-permute-start(bf16[1,128,768]{2,1,0:T(8,128)(2,1)S(1)} %fusion.28), channel_id=1, source_target_pairs={{0,16},{8,24},{16,0},{24,8},{1,17},{9,25},{17,1},{25,9},{2,18},{10... | collective-permute-start | bytes 589832 | tf_op jit(solution)/shard_map/ppermute | solution.py:96
  6.5 12.2 %all-to-all-start = ((bf16[4,192,128]{2,1,0:T(8,128)(2,1)}), bf16[4,192,128]{2,1,0:T(8,128)(2,1)S(1)}, u32[]{:S(2)}, u32[]{:S(2)}) async-start(bf16[4,192,128]{2,1,0:T(8,128)(2,1)} %bitcast.10), calls=%async_computation | async-start | bytes 393216 | tf_op jit(solution)/shard_map/all_to_all | solution.py:125
  10.8 9.4 %collective-permute-start.2 = (bf16[64,768]{1,0:T(8,128)(2,1)S(1)}, bf16[64,768]{1,0:T(8,128)(2,1)S(1)}, u32[]{:S(2)}, u32[]{:S(2)}) collective-permute-start(bf16[64,768]{1,0:T(8,128)(2,1)S(1)} %get-tuple-element.25), channel_id=1, source_target_pairs={{8,16},{16,8},{9,17},{17,9},{10,18},{18,10},{11,19},{19,11},{12,20... | collective-permute-start | bytes 294920 | tf_op jit(solution)/shard_map/ppermute | solution.py:103
  13.0 4.9 %collective-permute-start.1 = (bf16[320,768]{1,0:T(8,128)(2,1)S(1)}, bf16[320,768]{1,0:T(8,128)(2,1)S(1)}, u32[]{:S(2)}, u32[]{:S(2)}) collective-permute-start(bf16[320,768]{1,0:T(8,128)(2,1)S(1)} %pad_maximum_fusion.1), channel_id=1, source_target_pairs={{0,8},{8,0},{16,24},{24,16},{1,9},{9,1},{17,25},{25,17},{2,10},{10... | collective-permute-start | bytes 1474568 | tf_op jit(solution)/shard_map/ppermute | solution.py:99
  20.1 0.9 %copy-start = (bf16[1,128,768]{2,1,0:T(8,128)(2,1)S(1)}, bf16[1,128,768]{2,1,0:T(8,128)(2,1)}, u32[]{:S(2)}) copy-start(bf16[1,128,768]{2,1,0:T(8,128)(2,1)} %param.5) | copy-start | bytes 589828
  21.0 2.7 %copy-start.1 = (bf16[768,2304]{1,0:T(8,128)(2,1)S(1)}, bf16[768,2304]{1,0:T(8,128)(2,1)}, u32[]{:S(2)}) copy-start(bf16[768,2304]{1,0:T(8,128)(2,1)} %param.6) | copy-start | bytes 10616836
  21.4 10.1 %collective-permute-start.4 = (f16[592,192]{1,0:T(8,128)(2,1)S(1)}, f16[592,192]{1,0:T(8,128)(2,1)S(1)}, u32[]{:S(2)}, u32[]{:S(2)}) collective-permute-start(f16[592,192]{1,0:T(8,128)(2,1)S(1)} %pad_maximum_fusion.5), channel_id=1, source_target_pairs={{0,1},{1,0},{2,3},{3,2},{4,5},{5,4},{6,7},{7,6},{8,9},{9,8},{10,11... | collective-permute-start | bytes 681992 | tf_op jit(solution)/shard_map/ppermute | solution.py:53
  23.2 14.3 %collective-permute-start.3 = (f16[592,192]{1,0:T(8,128)(2,1)S(1)}, f16[592,192]{1,0:T(8,128)(2,1)S(1)}, u32[]{:S(2)}, u32[]{:S(2)}) collective-permute-start(f16[592,192]{1,0:T(8,128)(2,1)S(1)} %pad_maximum_fusion.4), channel_id=1, source_target_pairs={{0,1},{1,0},{2,3},{3,2},{4,5},{5,4},{6,7},{7,6},{8,9},{9,8},{10,11... | collective-permute-start | bytes 681992 | tf_op jit(solution)/shard_map/ppermute | solution.py:53
  38.0 14.3 %collective-permute-start.7 = (f16[304,192]{1,0:T(8,128)(2,1)S(1)}, f16[304,192]{1,0:T(8,128)(2,1)S(1)}, u32[]{:S(2)}, u32[]{:S(2)}) collective-permute-start(f16[304,192]{1,0:T(8,128)(2,1)S(1)} %get-tuple-element.29), channel_id=1, source_target_pairs={{0,4},{1,5},{2,6},{3,7},{4,0},{5,1},{6,2},{7,3},{8,12},{9,13},{10,... | collective-permute-start | bytes 350216 | tf_op jit(solution)/shard_map/ppermute | solution.py:53
  41.7 10.7 %collective-permute-start.6 = (f16[304,192]{1,0:T(8,128)(2,1)S(1)}, f16[304,192]{1,0:T(8,128)(2,1)S(1)}, u32[]{:S(2)}, u32[]{:S(2)}) collective-permute-start(f16[304,192]{1,0:T(8,128)(2,1)S(1)} %get-tuple-element.28), channel_id=1, source_target_pairs={{0,2},{1,3},{2,4},{3,5},{4,6},{5,7},{6,0},{7,1},{8,10},{9,11},{10,... | collective-permute-start | bytes 350216 | tf_op jit(solution)/shard_map/ppermute | solution.py:53
  43.3 10.5 %collective-permute-start.5 = (f16[304,192]{1,0:T(8,128)(2,1)S(1)}, f16[304,192]{1,0:T(8,128)(2,1)S(1)}, u32[]{:S(2)}, u32[]{:S(2)}) collective-permute-start(f16[304,192]{1,0:T(8,128)(2,1)S(1)} %get-tuple-element.27), channel_id=1, source_target_pairs={{0,6},{1,7},{2,0},{3,1},{4,2},{5,3},{6,4},{7,5},{8,14},{9,15},{10,... | collective-permute-start | bytes 350216 | tf_op jit(solution)/shard_map/ppermute | solution.py:53
where the time goes:
time: 55.1 us; the launch traced here: 54.8 us
  waiting for transfers between devices  22.4 us (41%)
  starting transfers between devices  19.1 us (35%)
  local copies, waits for them, and re-layouts  5.33 us (10%)
  other arithmetic  4.04 us (7%)
  matrix products  2.96 us (5%)
  between operations  0.93 us (2%)
    ppermute x5, waiting for transfers between devices, send(): arrived = lax.ppermute(encode(values, exponent), 'batch', perm)  21.1 us
    ppermute x5, starting transfers between devices, send(): arrived = lax.ppermute(encode(values, exponent), 'batch', perm)  8.65 us
    ppermute x1, starting transfers between devices, gather_over_seq(): incoming = lax.ppermute(outgoing, 'seq', [(i, i ^ 1) for i in range(count)])  3.39 us
    all_to_all x1, starting transfers between devices, body(): arrived = lax.all_to_all(channels, 'seq', 0, 0, tiled=True)  3.37 us
    ppermute x1, starting transfers between devices, gather_over_seq(): stack = jnp.concatenate([stack, lax.ppermute(stack, 'seq', pairs)], axis=0)  3.03 us
    transpose x1, local copies, waits for them, and re-layouts, body(): channels = cotangent[0].T.reshape(seq_count, -1, length)  1.74 us
    dot_general x3, matrix products, body(): jnp.dot(window, weight[:, tap_index * in_width:(tap_index + 1) * in_width...  1.66 us
    unnamed x7, local copies, waits for them, and re-layouts  1.57 us
  transfers between devices with their start and end apart: 9, of which 5 were waited for; matrix products, arithmetic and copies ran while one was open for 16% of the time, Pallas kernels for 0%

commit v1 on v0

--- a/solution.py
+++ b/solution.py
@@ -9,6 +9,18 @@
 TAP_SPACING = 64
 HEADROOM = 12.0
 TAG = 16
+
+
+def split_up(shard, dim, devices):
+    shape = shard.shape
+    tiles = shard.reshape(*shape[:dim], devices, shape[dim] // devices, *shape[dim + 1 :])
+    return jnp.moveaxis(tiles, dim, 0)
+
+
+def in_order(pieces, dim):
+    dims = list(pieces.shape[1:])
+    dims[dim] *= pieces.shape[0]
+    return jnp.moveaxis(pieces, 0, dim).reshape(dims)
 
 
 def extended_2(x, sides, width):
@@ -122,7 +134,15 @@
     counted = batch_count * inputs.shape[0] * length * seq_count
     factor = 1.0 / math.sqrt(float(counted))
     channels = cotangent[0].T.reshape(seq_count, -1, length)
-    arrived = lax.all_to_all(channels, "seq", 0, 0, tiled=True)
+    size, index = (lax.axis_size("seq"), lax.axis_index("seq"))
+    parts = split_up(channels, 0, size)
+    filled = parts
+    for step in range(1, size):
+        target_2, source = ((index + step) % size, (index - step) % size)
+        sent = lax.dynamic_index_in_dim(parts, target_2, 0)
+        got = lax.ppermute(sent, "seq", [(i_2, (i_2 + step) % size) for i_2 in range(size)])
+        filled = lax.dynamic_update_slice_in_dim(filled, got, source, axis=0)
+    arrived = in_order(filled, 0)
     own_rows = arrived.shape[1]
     owned = jnp.transpose(arrived, (1, 0, 2)).reshape(own_rows, -1)
     if seq_count >= 2 and seq_count & seq_count - 1 == 0:

time: 55.1 us -> 53.1 us (0.964)
  starting transfers between devices: 19.1 us -> 16.3 us
  local copies, waits for them, and re-layouts: 5.33 us -> 6.75 us
  other arithmetic: 4.04 us -> 3.42 us
    ppermute x0 -> x3, starting transfers between devices: none -> 3.89 us  [body(): lax.ppermute(sent, 'seq', [(i_2, (i_2 + step) % size) for i_2 in range(si...]
    all_to_all x1 -> x0, starting transfers between devices: 3.37 us -> none  [body(): arrived = lax.all_to_all(channels, 'seq', 0, 0, tiled=True)]
    ppermute x1, starting transfers between devices: 3.39 us -> 0.07 us  [gather_over_seq(): incoming = lax.ppermute(outgoing, 'seq', [(i, i ^ 1) for i in range(count)])]
    dynamic_update_slice x0 -> x3, local copies, waits for them, and re-layouts: none -> 2.44 us  [body(): filled = lax.dynamic_update_slice_in_dim(filled, got, source, axis=0)]
    transpose x1 -> x0, local copies, waits for them, and re-layouts: 1.74 us -> none  [body(): channels = cotangent[0].T.reshape(seq_count, -1, length)]
    select_n x1, other arithmetic: 0.96 us -> 0.13 us  [gather_over_seq(): far = lax.ppermute(jnp.where(odd, last, first), 'seq', across)]
    dynamic_slice x0 -> x1, local copies, waits for them, and re-layouts: none -> 0.66 us  [body(): sent = lax.dynamic_index_in_dim(parts, target_2, 0)]
    gather x1, local copies, waits for them, and re-layouts: 1.3 us -> 0.64 us  [gather_over_seq(): order = reverse[jnp.bitwise_xor(me, jnp.arange(count, dtype=jnp.int32))]]
  transfers between devices with their start and end apart: 9 -> 11, of which waited for: 5 -> 5; matrix products, arithmetic and copies ran while one was open for 16% -> 15% of each run, Pallas kernels for 0% -> 0%
where the time goes in v1:
time: 53.1 us; the launch traced here: 52.7 us
  waiting for transfers between devices  22 us (41%)
  starting transfers between devices  16.3 us (31%)
  local copies, waits for them, and re-layouts  6.75 us (13%)
  other arithmetic  3.42 us (6%)
  matrix products  3.12 us (6%)
  between operations  1.16 us (2%)
    ppermute x5, waiting for transfers between devices, send(): arrived = lax.ppermute(encode(values, exponent), 'batch', perm)  20.5 us
    ppermute x5, starting transfers between devices, send(): arrived = lax.ppermute(encode(values, exponent), 'batch', perm)  8.64 us
    ppermute x3, starting transfers between devices, body(): lax.ppermute(sent, 'seq', [(i_2, (i_2 + step) % size) for i_2 in range(si...  3.89 us
    ppermute x1, starting transfers between devices, gather_over_seq(): stack = jnp.concatenate([stack, lax.ppermute(stack, 'seq', pairs)], axis=0)  3.03 us
    dynamic_update_slice x3, local copies, waits for them, and re-layouts, body(): filled = lax.dynamic_update_slice_in_dim(filled, got, source, axis=0)  2.44 us
    unnamed x9, local copies, waits for them, and re-layouts  2.15 us
    dot_general x3, matrix products, body(): jnp.dot(window, weight[:, tap_index * in_width:(tap_index + 1) * in_width...  1.82 us
    ppermute x1, waiting for transfers between devices, gather_over_seq(): incoming = lax.ppermute(outgoing, 'seq', [(i, i ^ 1) for i in range(count)])  1.44 us
  transfers between devices with their start and end apart: 11, of which 5 were waited for; matrix products, arithmetic and copies ran while one was open for 15% of the time, Pallas kernels for 0%

profile of v1, /device:TPU:0, one launch (start us, length us, event | category | flops | bytes accessed | tf_op | source)
XLA Modules:
  0.0 52.7 jit_solution(9426001283891368395)
XLA Ops:
  0.7 1.1 %fusion.28 = bf16[1,128,768]{2,1,0:T(8,128)(2,1)S(1)} fusion(bf16[1,128,768]{2,1,0:T(8,128)(2,1)} %param.4), kind=kLoop, calls=%fused_computation.47 | loop fusion | flops 589824 | bytes 393216 | tf_op jit(solution)/shard_map/convert_element_type | solution.py:131
  1.7 3.0 %collective-permute-start = (bf16[1,128,768]{2,1,0:T(8,128)(2,1)S(1)}, bf16[1,128,768]{2,1,0:T(8,128)(2,1)S(1)}, u32[]{:S(2)}, u32[]{:S(2)}) collective-permute-start(bf16[1,128,768]{2,1,0:T(8,128)(2,1)S(1)} %fusion.28), channel_id=1, source_target_pairs={{0,16},{8,24},{16,0},{24,8},{1,17},{9,25},{17,1},{25,9},{2,18},{10... | collective-permute-start | bytes 589832 | tf_op jit(solution)/shard_map/ppermute | solution.py:108
  4.8 1.1 %copy.47 = bf16[1,128,768]{1,2,0:T(8,128)(2,1)S(1)} copy(bf16[1,128,768]{2,1,0:T(8,128)(2,1)} %param.5) | data formatting | bytes 393216 | tf_op args[1]
  6.0 0.7 %collective-permute-start.5 = (bf16[64,768]{0,1:T(8,128)(2,1)S(1)}, bf16[64,768]{0,1:T(8,128)(2,1)S(1)}, u32[]{:S(2)}, u32[]{:S(2)}) collective-permute-start(bf16[64,768]{0,1:T(8,128)(2,1)S(1)} %get-tuple-element.29), channel_id=1, source_target_pairs={{8,16},{16,8},{9,17},{17,9},{10,18},{18,10},{11,19},{19,11},{12,20... | collective-permute-start | bytes 294920 | tf_op jit(solution)/shard_map/ppermute | solution.py:115
  6.7 0.7 %constant_dynamic-slice_fusion.2 = (bf16[1,1,192,128]{3,2,1,0:T(8,128)(2,1)}, bf16[1,1,192,128]{3,2,1,0:T(8,128)(2,1)}, bf16[1,1,192,128]{3,2,1,0:T(8,128)(2,1)}) fusion(bf16[4,1,192,128]{3,2,1,0:T(8,128)(2,1)S(1)} %bitcast.132, s32[]{:T(128)S(6)} %select_n.168, s32[]{:T(128)S(6)} %select_n.164, s32[]{:T(128)S(6)} %select_n.160), kind=kLoop, calls=%fused_computation.87 | loop fusion | bytes 294924 | tf_op jit(solution)/shard_map/jit(dynamic_index_in_dim)/dynamic_slice | solution.py:142
  7.4 1.4 %collective-permute-start.2 = (bf16[1,1,192,128]{3,2,1,0:T(8,128)(2,1)}, bf16[1,1,192,128]{3,2,1,0:T(8,128)(2,1)}, u32[]{:S(2)}, u32[]{:S(2)}) collective-permute-start(bf16[1,1,192,128]{3,2,1,0:T(8,128)(2,1)} %get-tuple-element.33), channel_id=1, source_target_pairs={{0,8},{8,16},{16,24},{24,0},{1,9},{9,17},{17,25},{25,1},{2,10},{10... | collective-permute-start | bytes 147464 | tf_op jit(solution)/shard_map/ppermute | solution.py:143
  8.8 1.1 %collective-permute-start.3 = (bf16[1,1,192,128]{3,2,1,0:T(8,128)(2,1)}, bf16[1,1,192,128]{3,2,1,0:T(8,128)(2,1)}, u32[]{:S(2)}, u32[]{:S(2)}) collective-permute-start(bf16[1,1,192,128]{3,2,1,0:T(8,128)(2,1)} %get-tuple-element.32), channel_id=1, source_target_pairs={{0,16},{8,24},{16,0},{24,8},{1,17},{9,25},{17,1},{25,9},{2,18},{10... | collective-permute-start | bytes 147464 | tf_op jit(solution)/shard_map/ppermute | solution.py:143
  9.8 1.4 %collective-permute-start.4 = (bf16[1,1,192,128]{3,2,1,0:T(8,128)(2,1)}, bf16[1,1,192,128]{3,2,1,0:T(8,128)(2,1)}, u32[]{:S(2)}, u32[]{:S(2)}) collective-permute-start(bf16[1,1,192,128]{3,2,1,0:T(8,128)(2,1)} %get-tuple-element.31), channel_id=1, source_target_pairs={{0,24},{8,0},{16,8},{24,16},{1,25},{9,1},{17,9},{25,17},{2,26},{10... | collective-permute-start | bytes 147464 | tf_op jit(solution)/shard_map/ppermute | solution.py:143
  11.4 0.6 %gather_fusion = s32[4]{0:T(128)S(1)} fusion(s32[4]{0:T(128)S(1)} %copy-done, s32[1024]{0:T(1024)S(1)} %pad_clamp_fusion.1), kind=kCustom, calls=%fused_computation | custom fusion | bytes 48 | tf_op jit(solution)/shard_map/gather | solution.py:120
  12.7 1.4 %collective-permute-done.1 = bf16[320,768]{1,0:T(8,128)(2,1)S(1)} collective-permute-done((bf16[320,768]{1,0:T(8,128)(2,1)S(1)}, bf16[320,768]{1,0:T(8,128)(2,1)S(1)}, u32[]{:S(2)}, u32[]{:S(2)}) %collective-permute-start.1) | collective-permute-done | bytes 491552 | tf_op jit(solution)/shard_map/ppermute | solution.py:111
  14.2 0.6 %gather_fusion.1 = bf16[4,128,768]{2,1,0:T(8,128)(2,1)S(1)} fusion(bf16[4,128,768]{2,1,0:T(8,128)(2,1)S(1)} %pad_maximum_fusion, s32[1024]{0:T(1024)S(1)} %pad_clamp_fusion), kind=kCustom, calls=%fused_computation.1 | custom fusion | bytes 1572880 | tf_op jit(solution)/shard_map/jit(_take)/gather | solution.py:121
  15.5 0.8 %bitcast_dynamic-update-slice_fusion.2 = bf16[4,192,128]{2,1,0:T(8,128)(2,1)S(1)} fusion(bf16[4,192,128]{2,1,0:T(8,128)(2,1)S(1)} %bitcast.134, s32[]{:T(128)S(6)} %select_n.162, bf16[1,1,192,128]{3,2,1,0:T(8,128)(2,1)} %collective-permute-done.2), kind=kLoop, calls=%fused_computation.82 | loop fusion | bytes 98308 | tf_op jit(solution)/shard_map/dynamic_update_slice | solution.py:144
  16.4 0.8 %bitcast_dynamic-update-slice_fusion.1 = bf16[4,192,128]{2,1,0:T(8,128)(2,1)S(1)} fusion(bf16[4,192,128]{2,1,0:T(8,128)(2,1)S(1)} %bitcast_dynamic-update-slice_fusion.2, s32[]{:T(128)S(6)} %select_n.166, bf16[1,1,192,128]{3,2,1,0:T(8,128)(2,1)} %collective-permute-done.3), kind=kLoop, calls=%fused_computation.81 | loop fusion | bytes 98308 | tf_op jit(solution)/shard_map/dynamic_update_slice | solution.py:144
  17.2 0.8 %bitcast_dynamic-update-slice_fusion = bf16[4,192,128]{2,1,0:T(8,128)(2,1)S(1)} fusion(bf16[4,192,128]{2,1,0:T(8,128)(2,1)S(1)} %bitcast_dynamic-update-slice_fusion.1, s32[]{:T(128)S(6)} %select_n.170, bf16[1,1,192,128]{3,2,1,0:T(8,128)(2,1)} %collective-permute-done.4), kind=kLoop, calls=%fused_computation.80 | loop fusion | bytes 98308 | tf_op jit(solution)/shard_map/dynamic_update_slice | solution.py:144
  19.9 1.6 %collective-permute-start.7 = (f16[592,192]{1,0:T(8,128)(2,1)S(1)}, f16[592,192]{1,0:T(8,128)(2,1)S(1)}, u32[]{:S(2)}, u32[]{:S(2)}) collective-permute-start(f16[592,192]{1,0:T(8,128)(2,1)S(1)} %pad_maximum_fusion.5), channel_id=1, source_target_pairs={{0,1},{1,0},{2,3},{3,2},{4,5},{5,4},{6,7},{7,6},{8,9},{9,8},{10,11... | collective-permute-start | bytes 681992 | tf_op jit(solution)/shard_map/ppermute | solution.py:65
  23.0 7.0 %collective-permute-done.7 = f16[592,192]{1,0:T(8,128)(2,1)S(1)} collective-permute-done((f16[592,192]{1,0:T(8,128)(2,1)S(1)}, f16[592,192]{1,0:T(8,128)(2,1)S(1)}, u32[]{:S(2)}, u32[]{:S(2)}) %collective-permute-start.7) | collective-permute-done | bytes 227360 | tf_op jit(solution)/shard_map/ppermute | solution.py:65
  30.0 5.6 %collective-permute-done.6 = f16[592,192]{1,0:T(8,128)(2,1)S(1)} collective-permute-done((f16[592,192]{1,0:T(8,128)(2,1)S(1)}, f16[592,192]{1,0:T(8,128)(2,1)S(1)}, u32[]{:S(2)}, u32[]{:S(2)}) %collective-permute-start.6) | collective-permute-done | bytes 227360 | tf_op jit(solution)/shard_map/ppermute | solution.py:65
  36.2 2.7 %collective-permute-start.10 = (f16[304,192]{1,0:T(8,128)(2,1)S(1)}, f16[304,192]{1,0:T(8,128)(2,1)S(1)}, u32[]{:S(2)}, u32[]{:S(2)}) collective-permute-start(f16[304,192]{1,0:T(8,128)(2,1)S(1)} %get-tuple-element.36), channel_id=1, source_target_pairs={{0,4},{1,5},{2,6},{3,7},{4,0},{5,1},{6,2},{7,3},{8,12},{9,13},{10,... | collective-permute-start | bytes 350216 | tf_op jit(solution)/shard_map/ppermute | solution.py:65
  38.9 1.0 %fusion.8 = bf16[1,128,768]{2,1,0:T(8,128)(2,1)} fusion(f32[128,768]{1,0:T(8,128)S(1)} %fusion.24, f32[128,768]{1,0:T(8,128)S(1)} %convolution_add_fusion.1, bf16[768,2304]{1,0:T(8,128)(2,1)S(1)} %copy-done.1, bf16[256,768]{0,1:T(8,128)(2,1)S(1)} %pad_maximum_fusion.3), kind=kOutput, calls=%fused_computation.14 | convolution fusion | flops 151289856 | bytes 2359296 | tf_op jit(solution)/shard_map/dot_general | solution.py:172
  40.0 1.6 %collective-permute-start.9 = (f16[304,192]{1,0:T(8,128)(2,1)S(1)}, f16[304,192]{1,0:T(8,128)(2,1)S(1)}, u32[]{:S(2)}, u32[]{:S(2)}) collective-permute-start(f16[304,192]{1,0:T(8,128)(2,1)S(1)} %get-tuple-element.35), channel_id=1, source_target_pairs={{0,2},{1,3},{2,4},{3,5},{4,6},{5,7},{6,0},{7,1},{8,10},{9,11},{10,... | collective-permute-start | bytes 350216 | tf_op jit(solution)/shard_map/ppermute | solution.py:65
  41.5 2.2 %collective-permute-start.8 = (f16[304,192]{1,0:T(8,128)(2,1)S(1)}, f16[304,192]{1,0:T(8,128)(2,1)S(1)}, u32[]{:S(2)}, u32[]{:S(2)}) collective-permute-start(f16[304,192]{1,0:T(8,128)(2,1)S(1)} %get-tuple-element.34), channel_id=1, source_target_pairs={{0,6},{1,7},{2,0},{3,1},{4,2},{5,3},{6,4},{7,5},{8,14},{9,15},{10,... | collective-permute-start | bytes 350216 | tf_op jit(solution)/shard_map/ppermute | solution.py:65
  43.8 6.6 %collective-permute-done.10 = f16[304,192]{1,0:T(8,128)(2,1)S(1)} collective-permute-done((f16[304,192]{1,0:T(8,128)(2,1)S(1)}, f16[304,192]{1,0:T(8,128)(2,1)S(1)}, u32[]{:S(2)}, u32[]{:S(2)}) %collective-permute-start.10) | collective-permute-done | bytes 116768 | tf_op jit(solution)/shard_map/ppermute | solution.py:65
  50.4 1.4 %collective-permute-done.8 = f16[304,192]{1,0:T(8,128)(2,1)S(1)} collective-permute-done((f16[304,192]{1,0:T(8,128)(2,1)S(1)}, f16[304,192]{1,0:T(8,128)(2,1)S(1)}, u32[]{:S(2)}, u32[]{:S(2)}) %collective-permute-start.8) | collective-permute-done | bytes 116768 | tf_op jit(solution)/shard_map/ppermute | solution.py:65
  51.9 0.9 %copy.61 = f32[192,288]{1,0:T(8,128)} copy(f32[192,288]{0,1:T(8,128)S(1)} %fusion.37) | data formatting | bytes 442368
  (60 shorter events, 5.5 us)
Async XLA Ops:
  0.6 10.8 %copy-start = (s32[4]{0:T(128)S(1)}, s32[4]{0:T(128)}, u32[]{:S(2)}) copy-start(s32[4]{0:T(128)} %constant.163.clone) | copy-start | bytes 52
  0.6 11.9 %copy-start.2 = (bf16[1,128,768]{2,1,0:T(8,128)(2,1)S(1)}, bf16[1,128,768]{2,1,0:T(8,128)(2,1)}, u32[]{:S(2)}) copy-start(bf16[1,128,768]{2,1,0:T(8,128)(2,1)} %param.4) | copy-start | bytes 589828
  1.7 10.4 %collective-permute-start = (bf16[1,128,768]{2,1,0:T(8,128)(2,1)S(1)}, bf16[1,128,768]{2,1,0:T(8,128)(2,1)S(1)}, u32[]{:S(2)}, u32[]{:S(2)}) collective-permute-start(bf16[1,128,768]{2,1,0:T(8,128)(2,1)S(1)} %fusion.28), channel_id=1, source_target_pairs={{0,16},{8,24},{16,0},{24,8},{1,17},{9,25},{17,1},{25,9},{2,18},{10... | collective-permute-start | bytes 589832 | tf_op jit(solution)/shard_map/ppermute | solution.py:108
  6.0 9.2 %collective-permute-start.5 = (bf16[64,768]{0,1:T(8,128)(2,1)S(1)}, bf16[64,768]{0,1:T(8,128)(2,1)S(1)}, u32[]{:S(2)}, u32[]{:S(2)}) collective-permute-start(bf16[64,768]{0,1:T(8,128)(2,1)S(1)} %get-tuple-element.29), channel_id=1, source_target_pairs={{8,16},{16,8},{9,17},{17,9},{10,18},{18,10},{11,19},{19,11},{12,20... | collective-permute-start | bytes 294920 | tf_op jit(solution)/shard_map/ppermute | solution.py:115
  7.4 8.1 %collective-permute-start.2 = (bf16[1,1,192,128]{3,2,1,0:T(8,128)(2,1)}, bf16[1,1,192,128]{3,2,1,0:T(8,128)(2,1)}, u32[]{:S(2)}, u32[]{:S(2)}) collective-permute-start(bf16[1,1,192,128]{3,2,1,0:T(8,128)(2,1)} %get-tuple-element.33), channel_id=1, source_target_pairs={{0,8},{8,16},{16,24},{24,0},{1,9},{9,17},{17,25},{25,1},{2,10},{10... | collective-permute-start | bytes 147464 | tf_op jit(solution)/shard_map/ppermute | solution.py:143
  8.8 7.6 %collective-permute-start.3 = (bf16[1,1,192,128]{3,2,1,0:T(8,128)(2,1)}, bf16[1,1,192,128]{3,2,1,0:T(8,128)(2,1)}, u32[]{:S(2)}, u32[]{:S(2)}) collective-permute-start(bf16[1,1,192,128]{3,2,1,0:T(8,128)(2,1)} %get-tuple-element.32), channel_id=1, source_target_pairs={{0,16},{8,24},{16,0},{24,8},{1,17},{9,25},{17,1},{25,9},{2,18},{10... | collective-permute-start | bytes 147464 | tf_op jit(solution)/shard_map/ppermute | solution.py:143
  9.8 7.3 %collective-permute-start.4 = (bf16[1,1,192,128]{3,2,1,0:T(8,128)(2,1)}, bf16[1,1,192,128]{3,2,1,0:T(8,128)(2,1)}, u32[]{:S(2)}, u32[]{:S(2)}) collective-permute-start(bf16[1,1,192,128]{3,2,1,0:T(8,128)(2,1)} %get-tuple-element.31), channel_id=1, source_target_pairs={{0,24},{8,0},{16,8},{24,16},{1,25},{9,1},{17,9},{25,17},{2,26},{10... | collective-permute-start | bytes 147464 | tf_op jit(solution)/shard_map/ppermute | solution.py:143
  12.2 1.9 %collective-permute-start.1 = (bf16[320,768]{1,0:T(8,128)(2,1)S(1)}, bf16[320,768]{1,0:T(8,128)(2,1)S(1)}, u32[]{:S(2)}, u32[]{:S(2)}) collective-permute-start(bf16[320,768]{1,0:T(8,128)(2,1)S(1)} %pad_maximum_fusion.1), channel_id=1, source_target_pairs={{0,8},{8,0},{16,24},{24,16},{1,9},{9,1},{17,25},{25,17},{2,10},{10... | collective-permute-start | bytes 1474568 | tf_op jit(solution)/shard_map/ppermute | solution.py:111
  19.5 2.7 %copy-start.1 = (bf16[768,2304]{1,0:T(8,128)(2,1)S(1)}, bf16[768,2304]{1,0:T(8,128)(2,1)}, u32[]{:S(2)}) copy-start(bf16[768,2304]{1,0:T(8,128)(2,1)} %param.6) | copy-start | bytes 10616836
  19.9 10.1 %collective-permute-start.7 = (f16[592,192]{1,0:T(8,128)(2,1)S(1)}, f16[592,192]{1,0:T(8,128)(2,1)S(1)}, u32[]{:S(2)}, u32[]{:S(2)}) collective-permute-start(f16[592,192]{1,0:T(8,128)(2,1)S(1)} %pad_maximum_fusion.5), channel_id=1, source_target_pairs={{0,1},{1,0},{2,3},{3,2},{4,5},{5,4},{6,7},{7,6},{8,9},{9,8},{10,11... | collective-permute-start | bytes 681992 | tf_op jit(solution)/shard_map/ppermute | solution.py:65
  21.6 14.0 %collective-permute-start.6 = (f16[592,192]{1,0:T(8,128)(2,1)S(1)}, f16[592,192]{1,0:T(8,128)(2,1)S(1)}, u32[]{:S(2)}, u32[]{:S(2)}) collective-permute-start(f16[592,192]{1,0:T(8,128)(2,1)S(1)} %pad_maximum_fusion.4), channel_id=1, source_target_pairs={{0,1},{1,0},{2,3},{3,2},{4,5},{5,4},{6,7},{7,6},{8,9},{9,8},{10,11... | collective-permute-start | bytes 681992 | tf_op jit(solution)/shard_map/ppermute | solution.py:65
  36.2 14.1 %collective-permute-start.10 = (f16[304,192]{1,0:T(8,128)(2,1)S(1)}, f16[304,192]{1,0:T(8,128)(2,1)S(1)}, u32[]{:S(2)}, u32[]{:S(2)}) collective-permute-start(f16[304,192]{1,0:T(8,128)(2,1)S(1)} %get-tuple-element.36), channel_id=1, source_target_pairs={{0,4},{1,5},{2,6},{3,7},{4,0},{5,1},{6,2},{7,3},{8,12},{9,13},{10,... | collective-permute-start | bytes 350216 | tf_op jit(solution)/shard_map/ppermute | solution.py:65
  40.0 10.4 %collective-permute-start.9 = (f16[304,192]{1,0:T(8,128)(2,1)S(1)}, f16[304,192]{1,0:T(8,128)(2,1)S(1)}, u32[]{:S(2)}, u32[]{:S(2)}) collective-permute-start(f16[304,192]{1,0:T(8,128)(2,1)S(1)} %get-tuple-element.35), channel_id=1, source_target_pairs={{0,2},{1,3},{2,4},{3,5},{4,6},{5,7},{6,0},{7,1},{8,10},{9,11},{10,... | collective-permute-start | bytes 350216 | tf_op jit(solution)/shard_map/ppermute | solution.py:65
  41.5 10.2 %collective-permute-start.8 = (f16[304,192]{1,0:T(8,128)(2,1)S(1)}, f16[304,192]{1,0:T(8,128)(2,1)S(1)}, u32[]{:S(2)}, u32[]{:S(2)}) collective-permute-start(f16[304,192]{1,0:T(8,128)(2,1)S(1)} %get-tuple-element.34), channel_id=1, source_target_pairs={{0,6},{1,7},{2,0},{3,1},{4,2},{5,3},{6,4},{7,5},{8,14},{9,15},{10,... | collective-permute-start | bytes 350216 | tf_op jit(solution)/shard_map/ppermute | solution.py:65
